TPU v7x, 128 devices: a whole 4x4x4 slice. The times are simulated.
128 devices in a mesh: child: 2 (over z_hi), row: 8 (over y, core), col: 8 (over x, z_lo).
Axes of the slice: x: 4, y: 4, z: 4 (z_hi: 2, z_lo: 2; z = z_hi * 2 + z_lo), core: 2. Of those that a mesh axis runs over, the one named last changes fastest.
Arguments:
- child_fronts: float32 [2, 8192, 8192], P('child', 'row', 'col')
- parent_front: float32 [12288, 12288], P('row', ('child', 'col')), may hold values from -6 to 6
- index_maps: int32 [2, 8192], replicated, may hold values from 0 to 12287, as said below
- orders: int32 [2], replicated, may hold values from 4096 to 8192, as said below
Outputs:
- assembled: float32 [12288, 12288], P('row', ('child', 'col'))
- panel_factor: float32 [2, 8192, 512], P('child', 'row')
Inputs may be any that keep to these rules, and one draw needn't show every extreme that they name: For each child, index_maps is one to one. Cut the child indices into aligned blocks of 8192 / 8 and the parent indices into 2 * 8 aligned slices of 12288 / (2 * 8): each block sends exactly 8192 / (2 * 8 * 8) of its indices into each slice. `orders`: one child's order is 8192.
All inputs are finite; a program needn't handle non-finite values.
Results may differ from a plain program's by a relative error of at most 0.0001.
Values sent between devices are 32-bit elements; how exact they have to be, the bound alone decides.
No kernel may reach another device: no remote copies, remote signals or barrier semaphores. Data moves between devices by JAX's collectives and lax.ppermute only.
A program may use at most 128 MiB of HBM per device.

v0:
```python
import jax
import jax.numpy as jnp
from jax import lax
from jax.sharding import PartitionSpec as P

PANEL = 512
FRONT = 8192


def from_root(value, axis, source):
    kept = jnp.where(lax.axis_index(axis) == source, value, 0).astype(value.dtype)
    return lax.psum(kept, axis)


def spread_sum(value, axis):
    count = lax.axis_size(axis)
    pieces = value.reshape(count, value.shape[0] // count, value.shape[1])
    arrived = lax.all_to_all(pieces, axis, 0, 0, tiled=True)
    return lax.all_gather(arrived.sum(0), axis, axis=0, tiled=True)


def from_first(value, axis, gather=True):
    count = lax.axis_size(axis)
    pieces = value.reshape(count, value.shape[0] // count, value.shape[1])
    arrived = lax.all_to_all(pieces, axis, 0, 0, tiled=True)
    if not gather:
        return arrived[0]
    return lax.all_gather(arrived[0], axis, axis=0, tiled=True)


def select_rows(parent_map, owner, width, count):
    everywhere = jnp.arange(FRONT, dtype=jnp.int32)
    keyed = jnp.where(parent_map // width == owner, everywhere, everywhere + FRONT)
    chosen = jnp.argsort(keyed)[:count]
    return parent_map[chosen] - owner * width


def invert_slots(slots, length):
    count = slots.shape[0]
    lookup = jnp.full((length,), count, jnp.int32)
    return lookup.at[slots].set(jnp.arange(count, dtype=jnp.int32))


def one_hot(order, size):
    positions = jnp.arange(size, dtype=jnp.int32)
    return (positions[:, None] == order[None, :]).astype(jnp.float32)


def exact_matmul(values, select):
    return jnp.dot(values, select, precision=lax.Precision.HIGHEST)


def factor_and_invert(matrix, size):
    count = matrix.shape[0] // size
    eye = jnp.eye(size, dtype=jnp.float32)
    high = lax.Precision.HIGHEST
    trailing = (matrix + matrix.T) * 0.5
    factor, inverse = ({}, {})
    for k in range(count):
        factor[k, k] = jnp.linalg.cholesky(trailing[:size, :size])
        inverse[k, k] = lax.linalg.triangular_solve(factor[k, k], eye, left_side=True, lower=True)
        if k + 1 < count:
            panel = jnp.dot(trailing[size:, :size], inverse[k, k].T, precision=high)
            for i in range(k + 1, count):
                factor[i, k] = panel[(i - k - 1) * size : (i - k) * size]
            trailing = trailing[size:, size:] - jnp.dot(panel, panel.T, precision=high)
    for i in range(count):
        for j in range(i - 1, -1, -1):
            total = sum((jnp.dot(factor[i, k], inverse[k, j], precision=high) for k in range(j, i)))
            inverse[i, j] = -jnp.dot(inverse[i, i], total, precision=high)
    zero = jnp.zeros((size, size), jnp.float32)

    def assemble(blocks):
        return jnp.concatenate(
            [
                jnp.concatenate([blocks[i, j] if j <= i else zero for j in range(count)], axis=1)
                for i in range(count)
            ]
        )

    return (assemble(factor), assemble(inverse))


def factor_panel(diag_factor, inverse, columns, global_rows, own_order):
    solved = jnp.dot(columns, inverse.T, precision=lax.Precision.HIGHEST)
    top_rows = jnp.pad(diag_factor, ((0, columns.shape[0] - PANEL), (0, 0)))
    result = jnp.where(global_rows[:, None] < PANEL, top_rows, solved)
    return jnp.where(global_rows[:, None] < own_order, result, jnp.float32(0.0))


def on_device(child_fronts, parent_front, index_maps, orders):
    block_here = child_fronts[0]
    rows_here, cols_here = block_here.shape
    child_index = lax.axis_index("child")
    row_index = lax.axis_index("row")
    col_index = lax.axis_index("col")
    n_row = lax.axis_size("row")
    n_col = lax.axis_size("col")
    own_map = lax.dynamic_index_in_dim(index_maps, child_index, 0, keepdims=False)
    own_order = lax.dynamic_index_in_dim(orders, child_index, 0, keepdims=False)
    global_rows = row_index * rows_here + jnp.arange(rows_here, dtype=jnp.int32)
    global_cols = col_index * cols_here + jnp.arange(cols_here, dtype=jnp.int32)
    panel_rows = rows_here // n_col
    first_piece = block_here[:panel_rows, :PANEL]
    for target in range(1, n_col):
        moved = lax.ppermute(
            block_here[target * panel_rows : (target + 1) * panel_rows, :PANEL],
            "col",
            [(0, target)],
        )
        first_piece = jnp.where(col_index == target, moved, first_piece)
    columns = lax.all_gather(first_piece, "col", axis=0, tiled=True)
    part_rows = rows_here // n_row
    own_piece = lax.dynamic_slice_in_dim(columns, col_index * part_rows, part_rows)
    pairs = [(n_col * a + b, n_col * b + a) for a in range(n_row) for b in range(n_col)]
    transposed_piece = lax.ppermute(own_piece, ("row", "col"), pairs)
    corner_rows = PANEL // n_row
    corner_piece = columns[:corner_rows]
    for target in range(1, n_row):
        moved = lax.ppermute(
            columns[target * corner_rows : (target + 1) * corner_rows], "row", [(0, target)]
        )
        corner_piece = jnp.where(row_index == target, moved, corner_piece)
    gathered = lax.all_gather(
        jnp.concatenate([transposed_piece, corner_piece]), "row", axis=0, tiled=False
    )
    other_columns = gathered[:, :part_rows].reshape(rows_here, PANEL)
    corner = gathered[:, part_rows:].reshape(PANEL, PANEL)
    diag_factor, inverse = factor_and_invert(corner, PANEL // 4)
    own_panel = factor_panel(diag_factor, inverse, columns, global_rows, own_order)
    other_panel = factor_panel(diag_factor, inverse, other_columns, global_cols, own_order)
    parent_rows, parent_cols = parent_front.shape
    row_map = lax.dynamic_slice_in_dim(own_map, row_index * rows_here, rows_here)
    col_map = lax.dynamic_slice_in_dim(own_map, col_index * cols_here, cols_here)
    row_keys = row_map // parent_rows * rows_here + jnp.arange(rows_here, dtype=jnp.int32)
    col_keys = col_map // parent_cols * cols_here + jnp.arange(cols_here, dtype=jnp.int32)
    col_order = jnp.argsort(col_keys)
    col_select = one_hot(col_order, cols_here)
    row_order = jnp.argsort(row_keys)
    live_rows = (global_rows >= PANEL) & (global_rows < own_order)
    live_cols = (global_cols >= PANEL) & (global_cols < own_order)
    update = block_here[row_order] - jnp.dot(
        own_panel[row_order], other_panel.T, precision=lax.Precision.HIGHEST
    )
    update = jnp.where(live_rows[row_order][:, None] & live_cols[None, :], update, jnp.float32(0.0))
    turned = jnp.einsum("qj,iq->ji", col_select, update, precision=lax.Precision.HIGHEST)
    part_cols = cols_here // (2 * n_col)
    pieces = (
        turned.reshape(2, n_col, part_cols, n_row, part_rows)
        .transpose(0, 3, 1, 2, 4)
        .reshape(-1, part_rows)
    )
    arrived = lax.all_to_all(
        pieces, ("child", "row", "col"), split_axis=0, concat_axis=0, tiled=True
    )
    arrived = arrived.reshape(2, n_row, n_col * part_cols, part_rows)
    col_owner = child_index * n_col + col_index
    assembled = parent_front
    for source in range(2):
        parent_map = index_maps[source]
        row_slots = select_rows(parent_map, row_index, parent_rows, rows_here)
        col_slots = select_rows(parent_map, col_owner, parent_cols, n_col * part_cols)
        row_lookup = invert_slots(row_slots, parent_rows)
        spread = jnp.einsum(
            "rqa,pq->rap",
            arrived[source],
            one_hot(col_slots, parent_cols),
            precision=lax.Precision.HIGHEST,
        ).reshape(rows_here, parent_cols)
        padded = jnp.pad(spread, ((0, 1), (0, 0)))
        assembled = assembled + jnp.take(padded, row_lookup, axis=0)
    return (assembled, own_panel[None])


def solution(mesh):
    in_specs = (P("child", "row", "col"), P("row", ("child", "col")), P(), P())
    out_specs = (P("row", ("child", "col")), P("child", "row", None))
    return jax.shard_map(
        on_device, mesh=mesh, in_specs=in_specs, out_specs=out_specs, check_vma=False
    )
```

profile of v0, /device:TPU:1, one launch (start us, length us, event | category | flops | bytes accessed | tf_op | source)
XLA Modules:
  0.0 416.2 jit_solution(1546975868611364427)
XLA Ops:
  8.8 4.4 %collective-permute-start.6 = (f32[128,512]{1,0:T(8,128)S(1)}, f32[128,512]{1,0:T(8,128)S(1)}, u32[]{:S(2)}, u32[]{:S(2)}) collective-permute-start(f32[128,512]{1,0:T(8,128)S(1)} %get-tuple-element.29), channel_id=1, source_target_pairs={{0,1},{8,9},{16,17},{24,25},{32,33},{40,41},{48,49},{56,57},{64,65... | collective-permute-start | bytes 786440 | tf_op jit(solution)/shard_map/ppermute | solution.py:106
  25.1 5.6 %collective-permute-done.3 = f32[128,512]{1,0:T(8,128)S(1)} collective-permute-done((f32[128,512]{1,0:T(8,128)S(1)}, f32[128,512]{1,0:T(8,128)S(1)}, u32[]{:S(2)}, u32[]{:S(2)}) %collective-permute-start.3) | collective-permute-done | bytes 262176 | tf_op jit(solution)/shard_map/ppermute | solution.py:106
  30.7 5.6 %collective-permute-done.2 = f32[128,512]{1,0:T(8,128)S(1)} collective-permute-done((f32[128,512]{1,0:T(8,128)S(1)}, f32[128,512]{1,0:T(8,128)S(1)}, u32[]{:S(2)}, u32[]{:S(2)}) %collective-permute-start.2) | collective-permute-done | bytes 262176 | tf_op jit(solution)/shard_map/ppermute | solution.py:106
  38.3 53.1 %all-gather.4.cloned.1.call-done = f32[1024,512]{1,0:T(8,128)} async-done(((f32[128,512]{1,0:T(8,128)}), f32[1024,512]{1,0:T(8,128)}) %all-gather.4.cloned.1.call-update) | async-done | bytes 2097168 | tf_op jit(solution)/shard_map/all_gather | solution.py:112
  99.8 10.2 %collective-permute-start.7 = (f32[128,512]{1,0:T(8,128)S(1)}, f32[128,512]{1,0:T(8,128)S(1)}, u32[]{:S(2)}, u32[]{:S(2)}) collective-permute-start(f32[128,512]{1,0:T(8,128)S(1)} %constant_dynamic-slice_fusion), channel_id=1, source_target_pairs={{0,0},{1,8},{2,16},{3,24},{4,32},{5,40},{6,48},{7,56},{8,1},{9,9},... | collective-permute-start | bytes 786440 | tf_op jit(solution)/shard_map/ppermute | solution.py:116
  121.7 8.5 %gather_fusion.1 = f32[1024,1024]{1,0:T(8,128)} fusion(f32[1024,1024]{1,0:T(8,128)} %bitcast.119, s32[1024]{0:T(1024)S(1)} %fusion.78), kind=kCustom, calls=%fused_computation.3 | custom fusion | bytes 8392704 | tf_op jit(solution)/shard_map/gather | solution.py:142
  130.8 7.0 %gather_fusion = pred[1024]{0:T(1024)(128)(4,1)S(1)} fusion(pred[1024]{0:T(1024)(128)(4,1)S(1)} %fusion.91, s32[1024]{0:T(1024)S(1)} %fusion.78), kind=kCustom, calls=%fused_computation.2 | custom fusion | bytes 6144 | tf_op jit(solution)/shard_map/gather | solution.py:145
  137.9 4.4 %sort.90 = (s32[1024]{0:T(1024)}, s32[1024]{0:T(1024)}) sort(s32[1024]{0:T(1024)S(1)} %get-tuple-element.62, s32[1024]{0:T(1024)S(1)} %iota.129), dimensions={0}, to_apply=%region_0.1 | sort | flops 10240 | bytes 16384 | tf_op jit(solution)/shard_map/jit(argsort)/sort | solution.py:137
  145.2 6.1 %all-gather.6.cloned.1.call-done = f32[1536,512]{1,0:T(8,128)} async-done(((f32[192,512]{1,0:T(8,128)}), f32[1536,512]{1,0:T(8,128)}) %all-gather.6.cloned.1.call-update) | async-done | bytes 3145744 | tf_op jit(solution)/shard_map/all_gather | solution.py:124
  156.5 11.7 %cholesky.74 = f32[128,128]{1,0:T(8,128)S(1)} custom-call(f32[128,128]{1,0:T(8,128)S(1)} %fusion.64), custom_call_target="Cholesky" | custom-call | tf_op jit(solution)/shard_map/jit(cholesky)/cholesky | solution.py:60
  169.7 9.8 %custom-call.8 = f32[1,128,128]{1,2,0:T(8,128)S(1)} custom-call(f32[1,128,128]{2,1,0:T(8,128)S(1)} %get-tuple-element.25), custom_call_target="InvertDiagBlocksLowerTriangular" | custom-call | tf_op jit(solution)/shard_map/triangular_solve/custom-call.0 | solution.py:61
  181.8 12.1 %cholesky.85 = f32[128,128]{1,0:T(8,128)S(1)} custom-call(f32[128,128]{1,0:T(8,128)S(1)} %fusion.62), custom_call_target="Cholesky" | custom-call | tf_op jit(solution)/shard_map/jit(cholesky)/cholesky | solution.py:60
  196.0 9.8 %custom-call.9 = f32[1,128,128]{1,2,0:T(8,128)S(1)} custom-call(f32[1,128,128]{2,1,0:T(8,128)S(1)} %get-tuple-element.23), custom_call_target="InvertDiagBlocksLowerTriangular" | custom-call | tf_op jit(solution)/shard_map/triangular_solve/custom-call.0 | solution.py:61
  207.7 11.7 %cholesky.96 = f32[128,128]{1,0:T(8,128)S(1)} custom-call(f32[128,128]{1,0:T(8,128)S(1)} %fusion.60), custom_call_target="Cholesky" | custom-call | tf_op jit(solution)/shard_map/jit(cholesky)/cholesky | solution.py:60
  221.3 9.8 %custom-call.10 = f32[1,128,128]{1,2,0:T(8,128)S(1)} custom-call(f32[1,128,128]{2,1,0:T(8,128)S(1)} %get-tuple-element.21), custom_call_target="InvertDiagBlocksLowerTriangular" | custom-call | tf_op jit(solution)/shard_map/triangular_solve/custom-call.0 | solution.py:61
  237.8 11.9 %cholesky.107 = f32[128,128]{1,0:T(8,128)S(1)} custom-call(f32[128,128]{1,0:T(8,128)S(1)} %fusion.58), custom_call_target="Cholesky" | custom-call | tf_op jit(solution)/shard_map/jit(cholesky)/cholesky | solution.py:60
  251.1 9.8 %custom-call.11 = f32[1,128,128]{1,2,0:T(8,128)S(1)} custom-call(f32[1,128,128]{2,1,0:T(8,128)S(1)} %get-tuple-element.19), custom_call_target="InvertDiagBlocksLowerTriangular" | custom-call | tf_op jit(solution)/shard_map/triangular_solve/custom-call.0 | solution.py:61
  264.7 5.8 %fusion.107 = f32[1024,512]{1,0:T(8,128)} fusion(f32[1024,512]{1,0:T(8,128)S(1)} %bitcast.130, f32[128,256]{1,0:T(8,128)S(1)} %broadcast.199, f32[128,128]{1,0:T(8,128)S(1)} %cholesky.75, f32[128,128]{1,0:T(8,128)S(1)} %fusion.45, f32[128,128]{1,0:T(8,128)S(1)} %copy.51, f32[128,128]{1,0:T(8,128)S(1)} %convolution_negate_fusion, ...), kind=kOutput, calls=%fused_computation.207 | convolution fusion | flops 3224633344 | bytes 5046272 | tf_op jit(solution)/shard_map/dot_general | solution.py:85
  270.8 4.9 %fusion.8 = f32[1024,512]{1,0:T(8,128)S(1)} fusion(f32[512,512]{1,0:T(8,128)S(1)} %fusion.21, f32[1024,512]{1,0:T(8,128)S(1)} %copy-done.4, pred[1024]{0:T(1024)(128)(4,1)S(1)} %copy-done.20, pred[1024]{0:T(1024)(128)(4,1)S(1)} %copy-done.21, f32[128,256]{1,0:T(8,128)S(1)} %broadcast.199, f32[128,128]{1,0:T(8,128)S(1)} %cholesky.75, ...), kind=kOutput, calls=%fused_computation.22 | convolution fusion | flops 3225681920 | bytes 6096896 | tf_op jit(solution)/shard_map/dot_general | solution.py:85
  275.7 4.9 %gather_fusion.2 = f32[1024,512]{1,0:T(8,128)} fusion(f32[1024,512]{1,0:T(8,128)S(1)} %fusion.8, s32[1024]{0:T(1024)S(1)} %fusion.78), kind=kCustom, calls=%fused_computation.4 | custom fusion | bytes 4198400 | tf_op jit(solution)/shard_map/gather | solution.py:143
  280.6 9.8 %fusion.10 = f32[1024,1024]{1,0:T(8,128)S(1)} fusion(f32[1024,512]{1,0:T(8,128)} %gather_fusion.2, f32[1024,512]{1,0:T(8,128)} %fusion.107, f32[512,512]{1,0:T(8,128)S(1)} %fusion.21, pred[1024]{0:T(1024)(128)(4,1)S(1)} %get-tuple-element.56, pred[1024]{0:T(1024)(128)(4,1)S(1)} %get-tuple-element.57), kind=kOutput, calls=%fused_computation.24 | convolution fusion | flops 6443499520 | bytes 9439232 | tf_op jit(solution)/shard_map/dot_general | solution.py:142
  290.5 9.0 %fusion.5 = f32[128,8,8,128]{3,1,2,0:T(8,128)S(1)} fusion(f32[1024,1024]{1,0:T(8,128)S(1)} %copy-done.2, f32[1024,1024]{1,0:T(8,128)S(1)} %fusion.10, s32[1024]{0:T(1024)S(1)} %copy-done.23, pred[1024]{0:T(1024)(128)(4,1)S(1)} %copy-done.22, pred[1024]{0:T(1024)(128)(4,1)S(1)} %gather_fusion), kind=kOutput, calls=%fused_computation.21 | convolution fusion | flops 12890144768 | bytes 12589056 | tf_op jit(solution)/shard_map/qj,iq->ji/dot_general | solution.py:146
  303.4 10.9 %all-to-all-start = ((f32[128,64,128]{2,1,0:T(8,128)}), f32[128,64,128]{2,1,0:T(8,128)}, u32[]{:S(2)}, u32[]{:S(2)}) async-start(f32[128,64,128]{2,1,0:T(8,128)} %bitcast.121), calls=%async_computation | async-start | bytes 8388608 | tf_op jit(solution)/shard_map/all_to_all | solution.py:153
  314.5 6.8 %sort.95 = (s32[8192]{0:T(1024)}, s32[8192]{0:T(1024)S(1)}) sort(s32[8192]{0:T(1024)S(1)} %get-tuple-element.54, s32[8192]{0:T(1024)S(1)} %iota.145), dimensions={0}, to_apply=%region_8.12 | sort | flops 106496 | bytes 131072 | tf_op jit(solution)/shard_map/jit(argsort)/sort | solution.py:34
  321.3 6.1 %gather_fusion.6 = s32[1024]{0:T(1024)S(1)} fusion(s32[8192]{0:T(1024)S(1)} %bitcast.115, s32[1024]{0:T(1024)S(1)} %fusion.80), kind=kCustom, calls=%fused_computation.8 | custom fusion | bytes 12288 | tf_op jit(solution)/shard_map/gather | solution.py:35
  327.4 6.8 %sort.94 = (s32[8192]{0:T(1024)}, s32[8192]{0:T(1024)S(1)}) sort(s32[8192]{0:T(1024)S(1)} %get-tuple-element.55, s32[8192]{0:T(1024)S(1)} %iota.143), dimensions={0}, to_apply=%region_7.11 | sort | flops 106496 | bytes 131072 | tf_op jit(solution)/shard_map/jit(argsort)/sort | solution.py:34
  337.4 6.8 %sort.92 = (s32[8192]{0:T(1024)}, s32[8192]{0:T(1024)S(1)}) sort(s32[8192]{0:T(1024)S(1)} %get-tuple-element.58, s32[8192]{0:T(1024)S(1)} %iota.138), dimensions={0}, to_apply=%region_4.7 | sort | flops 106496 | bytes 131072 | tf_op jit(solution)/shard_map/jit(argsort)/sort | solution.py:34
  347.5 6.8 %sort.93 = (s32[8192]{0:T(1024)}, s32[8192]{0:T(1024)S(1)}) sort(s32[8192]{0:T(1024)S(1)} %get-tuple-element.59, s32[8192]{0:T(1024)S(1)} %iota.140), dimensions={0}, to_apply=%region_5.8 | sort | flops 106496 | bytes 131072 | tf_op jit(solution)/shard_map/jit(argsort)/sort | solution.py:34
  354.3 6.1 %gather_fusion.4 = s32[1024]{0:T(1024)S(1)} fusion(s32[8192]{0:T(1024)S(1)} %bitcast.113, s32[1024]{0:T(1024)S(1)} %fusion.79), kind=kCustom, calls=%fused_computation.6 | custom fusion | bytes 12288 | tf_op jit(solution)/shard_map/gather | solution.py:35
  386.8 8.6 %gather_fusion.7 = f32[1536,768]{1,0:T(8,128)} fusion(f32[1025,768]{1,0:T(8,128)} %pad.15, s32[2048]{0:T(1024)S(1)} %pad_clamp_fusion.1), kind=kCustom, calls=%fused_computation.clone | custom fusion | bytes 9443328 | tf_op jit(solution)/shard_map/jit(_take)/gather | solution.py:171
  395.4 5.5 %gather_fusion.8 = f32[1536,768]{1,0:T(8,128)} fusion(f32[1025,768]{1,0:T(8,128)S(1)} %pad.16, s32[2048]{0:T(1024)S(1)} %pad_clamp_fusion), kind=kCustom, calls=%fused_computation.1.clone | custom fusion | bytes 9443328 | tf_op jit(solution)/shard_map/jit(_take)/gather | solution.py:171
  400.9 8.0 %select_add_fusion = f32[1536,768]{1,0:T(8,128)} fusion(f32[1536,768]{1,0:T(8,128)} %gather_fusion.8, f32[1536,768]{1,0:T(8,128)} %param.10, f32[1536,768]{1,0:T(8,128)} %gather_fusion.7, pred[1536]{0:T(1024)(128)(4,1)S(1)} %compare_and_fusion, pred[1536]{0:T(1024)(128)(4,1)S(1)} %compare_and_fusion.1), kind=kLoop, calls=%fused_computation.11 | loop fusion | flops 4718592 | bytes 18877440 | tf_op jit(solution)/shard_map/add | solution.py:171
  (205 shorter events, 101.9 us)
Async XLA Ops:
  7.2 84.2 %all-gather.4.cloned.1.call-start = ((), (), s32[]{:S(2)}) async-start(), calls=%async_computation.1 | async-start | bytes 2359296 | tf_op jit(solution)/shard_map/all_gather | solution.py:112
  8.8 9.7 %collective-permute-start.6 = (f32[128,512]{1,0:T(8,128)S(1)}, f32[128,512]{1,0:T(8,128)S(1)}, u32[]{:S(2)}, u32[]{:S(2)}) collective-permute-start(f32[128,512]{1,0:T(8,128)S(1)} %get-tuple-element.29), channel_id=1, source_target_pairs={{0,1},{8,9},{16,17},{24,25},{32,33},{40,41},{48,49},{56,57},{64,65... | collective-permute-start | bytes 786440 | tf_op jit(solution)/shard_map/ppermute | solution.py:106
  13.2 6.6 %collective-permute-start.5 = (f32[128,512]{1,0:T(8,128)S(1)}, f32[128,512]{1,0:T(8,128)S(1)}, u32[]{:S(2)}, u32[]{:S(2)}) collective-permute-start(f32[128,512]{1,0:T(8,128)S(1)} %get-tuple-element.30), channel_id=1, source_target_pairs={{0,2},{8,10},{16,18},{24,26},{32,34},{40,42},{48,50},{56,58},{64,6... | collective-permute-start | bytes 786440 | tf_op jit(solution)/shard_map/ppermute | solution.py:106
  14.5 10.6 %collective-permute-start.4 = (f32[128,512]{1,0:T(8,128)S(1)}, f32[128,512]{1,0:T(8,128)S(1)}, u32[]{:S(2)}, u32[]{:S(2)}) collective-permute-start(f32[128,512]{1,0:T(8,128)S(1)} %get-tuple-element.31), channel_id=1, source_target_pairs={{0,3},{8,11},{16,19},{24,27},{32,35},{40,43},{48,51},{56,59},{64,6... | collective-permute-start | bytes 786440 | tf_op jit(solution)/shard_map/ppermute | solution.py:106
  15.8 14.9 %collective-permute-start.3 = (f32[128,512]{1,0:T(8,128)S(1)}, f32[128,512]{1,0:T(8,128)S(1)}, u32[]{:S(2)}, u32[]{:S(2)}) collective-permute-start(f32[128,512]{1,0:T(8,128)S(1)} %get-tuple-element.32), channel_id=1, source_target_pairs={{0,4},{8,12},{16,20},{24,28},{32,36},{40,44},{48,52},{56,60},{64,6... | collective-permute-start | bytes 786440 | tf_op jit(solution)/shard_map/ppermute | solution.py:106
  17.1 19.2 %collective-permute-start.2 = (f32[128,512]{1,0:T(8,128)S(1)}, f32[128,512]{1,0:T(8,128)S(1)}, u32[]{:S(2)}, u32[]{:S(2)}) collective-permute-start(f32[128,512]{1,0:T(8,128)S(1)} %get-tuple-element.33), channel_id=1, source_target_pairs={{0,5},{8,13},{16,21},{24,29},{32,37},{40,45},{48,53},{56,61},{64,6... | collective-permute-start | bytes 786440 | tf_op jit(solution)/shard_map/ppermute | solution.py:106
  18.5 17.8 %collective-permute-start.1 = (f32[128,512]{1,0:T(8,128)S(1)}, f32[128,512]{1,0:T(8,128)S(1)}, u32[]{:S(2)}, u32[]{:S(2)}) collective-permute-start(f32[128,512]{1,0:T(8,128)S(1)} %get-tuple-element.34), channel_id=1, source_target_pairs={{0,6},{8,14},{16,22},{24,30},{32,38},{40,46},{48,54},{56,62},{64,7... | collective-permute-start | bytes 786440 | tf_op jit(solution)/shard_map/ppermute | solution.py:106
  19.8 16.5 %collective-permute-start = (f32[128,512]{1,0:T(8,128)S(1)}, f32[128,512]{1,0:T(8,128)S(1)}, u32[]{:S(2)}, u32[]{:S(2)}) collective-permute-start(f32[128,512]{1,0:T(8,128)S(1)} %get-tuple-element.35), channel_id=1, source_target_pairs={{0,7},{8,15},{16,23},{24,31},{32,39},{40,47},{48,55},{56,63},{64,7... | collective-permute-start | bytes 786440 | tf_op jit(solution)/shard_map/ppermute | solution.py:106
  38.2 76.6 %copy-start.24 = (s32[2]{0:T(128)S(1)}, s32[2]{0:T(128)}, u32[]{:S(2)}) copy-start(s32[2]{0:T(128)} %param.12) | copy-start | bytes 28
  38.2 113.1 %all-gather.6.cloned.1.call-start = ((), (), s32[]{:S(2)}) async-start(), calls=%async_computation.2 | async-start | bytes 3538944 | tf_op jit(solution)/shard_map/all_gather | solution.py:124
  92.7 4.8 %collective-permute-start.14 = (f32[64,512]{1,0:T(8,128)S(1)}, f32[64,512]{1,0:T(8,128)S(1)}, u32[]{:S(2)}, u32[]{:S(2)}) collective-permute-start(f32[64,512]{1,0:T(8,128)S(1)} %get-tuple-element.36), channel_id=1, source_target_pairs={{0,8},{1,9},{2,10},{3,11},{4,12},{5,13},{6,14},{7,15},{64,72},{65,... | collective-permute-start | bytes 393224 | tf_op jit(solution)/shard_map/ppermute | solution.py:120
  94.0 4.2 %collective-permute-start.13 = (f32[64,512]{1,0:T(8,128)S(1)}, f32[64,512]{1,0:T(8,128)S(1)}, u32[]{:S(2)}, u32[]{:S(2)}) collective-permute-start(f32[64,512]{1,0:T(8,128)S(1)} %get-tuple-element.37), channel_id=1, source_target_pairs={{0,16},{1,17},{2,18},{3,19},{4,20},{5,21},{6,22},{7,23},{64,80},{6... | collective-permute-start | bytes 393224 | tf_op jit(solution)/shard_map/ppermute | solution.py:120
  94.7 5.2 %collective-permute-start.12 = (f32[64,512]{1,0:T(8,128)S(1)}, f32[64,512]{1,0:T(8,128)S(1)}, u32[]{:S(2)}, u32[]{:S(2)}) collective-permute-start(f32[64,512]{1,0:T(8,128)S(1)} %get-tuple-element.38), channel_id=1, source_target_pairs={{0,24},{1,25},{2,26},{3,27},{4,28},{5,29},{6,30},{7,31},{64,88},{6... | collective-permute-start | bytes 393224 | tf_op jit(solution)/shard_map/ppermute | solution.py:120
  95.3 14.7 %collective-permute-start.11 = (f32[64,512]{1,0:T(8,128)S(1)}, f32[64,512]{1,0:T(8,128)S(1)}, u32[]{:S(2)}, u32[]{:S(2)}) collective-permute-start(f32[64,512]{1,0:T(8,128)S(1)} %get-tuple-element.39), channel_id=1, source_target_pairs={{0,32},{1,33},{2,34},{3,35},{4,36},{5,37},{6,38},{7,39},{64,96},{6... | collective-permute-start | bytes 393224 | tf_op jit(solution)/shard_map/ppermute | solution.py:120
  96.0 14.0 %collective-permute-start.10 = (f32[64,512]{1,0:T(8,128)S(1)}, f32[64,512]{1,0:T(8,128)S(1)}, u32[]{:S(2)}, u32[]{:S(2)}) collective-permute-start(f32[64,512]{1,0:T(8,128)S(1)} %get-tuple-element.40), channel_id=1, source_target_pairs={{0,40},{1,41},{2,42},{3,43},{4,44},{5,45},{6,46},{7,47},{64,104},{... | collective-permute-start | bytes 393224 | tf_op jit(solution)/shard_map/ppermute | solution.py:120
  97.5 12.6 %collective-permute-start.9 = (f32[64,512]{1,0:T(8,128)S(1)}, f32[64,512]{1,0:T(8,128)S(1)}, u32[]{:S(2)}, u32[]{:S(2)}) collective-permute-start(f32[64,512]{1,0:T(8,128)S(1)} %get-tuple-element.41), channel_id=1, source_target_pairs={{0,48},{1,49},{2,50},{3,51},{4,52},{5,53},{6,54},{7,55},{64,112},{... | collective-permute-start | bytes 393224 | tf_op jit(solution)/shard_map/ppermute | solution.py:120
  98.2 11.9 %collective-permute-start.8 = (f32[64,512]{1,0:T(8,128)S(1)}, f32[64,512]{1,0:T(8,128)S(1)}, u32[]{:S(2)}, u32[]{:S(2)}) collective-permute-start(f32[64,512]{1,0:T(8,128)S(1)} %get-tuple-element.42), channel_id=1, source_target_pairs={{0,56},{1,57},{2,58},{3,59},{4,60},{5,61},{6,62},{7,63},{64,120},{... | collective-permute-start | bytes 393224 | tf_op jit(solution)/shard_map/ppermute | solution.py:120
  99.8 14.2 %collective-permute-start.7 = (f32[128,512]{1,0:T(8,128)S(1)}, f32[128,512]{1,0:T(8,128)S(1)}, u32[]{:S(2)}, u32[]{:S(2)}) collective-permute-start(f32[128,512]{1,0:T(8,128)S(1)} %constant_dynamic-slice_fusion), channel_id=1, source_target_pairs={{0,0},{1,8},{2,16},{3,24},{4,32},{5,40},{6,48},{7,56},{8,1},{9,9},... | collective-permute-start | bytes 786440 | tf_op jit(solution)/shard_map/ppermute | solution.py:116
  234.3 30.2 %copy-start.3 = (f32[8,128,512]{2,1,0:T(8,128)S(1)}, f32[8,128,512]{2,1,0:T(8,128)}, u32[]{:S(2)}) copy-start(f32[8,128,512]{2,1,0:T(8,128)} %slice.219) | copy-start | bytes 6291460
  261.3 9.2 %copy-start.19 = (f32[128,128]{1,0:T(8,128)}, f32[128,128]{1,0:T(8,128)S(1)}, u32[]{:S(2)}) copy-start(f32[128,128]{1,0:T(8,128)S(1)} %copy.51) | copy-start | bytes 196612
  261.9 8.6 %copy-start.14 = (f32[128,128]{1,0:T(8,128)}, f32[128,128]{1,0:T(8,128)S(1)}, u32[]{:S(2)}) copy-start(f32[128,128]{1,0:T(8,128)S(1)} %convolution_negate_fusion.2) | copy-start | bytes 196612
  262.2 8.3 %copy-start.15 = (f32[128,128]{1,0:T(8,128)}, f32[128,128]{1,0:T(8,128)S(1)}, u32[]{:S(2)}) copy-start(f32[128,128]{1,0:T(8,128)S(1)} %convolution_negate_fusion) | copy-start | bytes 196612
  263.1 7.5 %copy-start.16 = (f32[128,128]{1,0:T(8,128)}, f32[128,128]{1,0:T(8,128)S(1)}, u32[]{:S(2)}) copy-start(f32[128,128]{1,0:T(8,128)S(1)} %convolution_negate_fusion.1) | copy-start | bytes 196612
  264.6 6.1 %copy-start.4 = (f32[1024,512]{1,0:T(8,128)S(1)}, f32[1024,512]{1,0:T(8,128)}, u32[]{:S(2)}) copy-start(f32[1024,512]{1,0:T(8,128)} %all-gather.4.cloned.1.call-done) | copy-start | bytes 6291460
  264.6 6.1 %copy-start.17 = (f32[128,128]{1,0:T(8,128)S(1)}, f32[128,128]{1,0:T(8,128)}, u32[]{:S(2)}) copy-start(f32[128,128]{1,0:T(8,128)} %copy.44) | copy-start | bytes 196612
  264.6 6.1 %copy-start.18 = (f32[128,128]{1,0:T(8,128)S(1)}, f32[128,128]{1,0:T(8,128)}, u32[]{:S(2)}) copy-start(f32[128,128]{1,0:T(8,128)} %copy.47) | copy-start | bytes 196612
  264.7 6.1 %copy-start.20 = (pred[1024]{0:T(1024)(128)(4,1)S(1)}, pred[1024]{0:T(1024)(128)(4,1)}, u32[]{:S(2)}) copy-start(pred[1024]{0:T(1024)(128)(4,1)} %get-tuple-element.60) | copy-start | bytes 3076
  280.6 9.9 %copy-start.2 = (f32[1024,1024]{1,0:T(8,128)S(1)}, f32[1024,1024]{1,0:T(8,128)}, u32[]{:S(2)}) copy-start(f32[1024,1024]{1,0:T(8,128)} %gather_fusion.1) | copy-start | bytes 12582916
  280.6 9.9 %copy-start.22 = (pred[1024]{0:T(1024)(128)(4,1)S(1)}, pred[1024]{0:T(1024)(128)(4,1)}, u32[]{:S(2)}) copy-start(pred[1024]{0:T(1024)(128)(4,1)} %fusion.92) | copy-start | bytes 3076
  280.6 9.9 %copy-start.23 = (s32[1024]{0:T(1024)S(1)}, s32[1024]{0:T(1024)}, u32[]{:S(2)}) copy-start(s32[1024]{0:T(1024)} %get-tuple-element.11) | copy-start | bytes 12292
  303.4 10.9 %copy-start.13 = (s32[2,8192]{1,0:T(2,128)S(1)}, s32[2,8192]{1,0:T(2,128)}, u32[]{:S(2)}) copy-start(s32[2,8192]{1,0:T(2,128)} %param.11) | copy-start | bytes 196612
  303.4 65.9 %all-to-all-start = ((f32[128,64,128]{2,1,0:T(8,128)}), f32[128,64,128]{2,1,0:T(8,128)}, u32[]{:S(2)}, u32[]{:S(2)}) async-start(f32[128,64,128]{2,1,0:T(8,128)} %bitcast.121), calls=%async_computation | async-start | bytes 8388608 | tf_op jit(solution)/shard_map/all_to_all | solution.py:153
  (11 other events, 60.6 us)
Sparse Core Ops, SparseCore 0:
  38.3 52.9 all-gather.3
  115.0 36.3 all-gather.5
where the time goes:
time: 420 us; the launch traced here: 416 us
  other arithmetic  147 us (35%)
  local copies, waits for them, and re-layouts  93 us (22%)
  waiting for transfers between devices  78.2 us (19%)
  matrix products  43.5 us (10%)
  starting transfers between devices  38.7 us (9%)
  between operations  15.8 us (4%)
    all_gather x1, waiting for transfers between devices, on_device(): columns = lax.all_gather(first_piece, 'col', axis=0, tiled=True)  53.1 us
    another operation x12, other arithmetic, factor_and_invert(): factor[k, k] = jnp.linalg.cholesky(trailing[:size, :size])  50.4 us
    another operation x8, other arithmetic, factor_and_invert(): lax.linalg.triangular_solve(factor[k, k], eye, left_side=True, lower=True)  43.2 us
    sort x4, other arithmetic, select_rows(): chosen = jnp.argsort(keyed)[:count]  27 us
    gather x4, local copies, waits for them, and re-layouts, select_rows(): return parent_map[chosen] - owner * width  18.8 us
    ppermute x7, waiting for transfers between devices, on_device(): lax.ppermute(block_here[target * panel_rows:(target + 1) * panel_rows, :P...  15.2 us
    gather x2, local copies, waits for them, and re-layouts, on_device(): assembled = assembled + jnp.take(padded, row_lookup, axis=0)  14.1 us
    ppermute x7, starting transfers between devices, on_device(): lax.ppermute(block_here[target * panel_rows:(target + 1) * panel_rows, :P...  12.2 us
  transfers between devices with their start and end apart: 18, of which 7 were waited for; matrix products, arithmetic and copies ran while one was open for 21% of the time, Pallas kernels for 0%

commit v1 on v0

--- a/solution.py
+++ b/solution.py
@@ -109,7 +109,8 @@
             [(0, target)],
         )
         first_piece = jnp.where(col_index == target, moved, first_piece)
-    columns = lax.all_gather(first_piece, "col", axis=0, tiled=True)
+    repeated = jnp.stack([first_piece] * lax.axis_size("col"))
+    columns = jnp.concatenate(lax.all_to_all(repeated, "col", 0, 0), axis=0)
     part_rows = rows_here // n_row
     own_piece = lax.dynamic_slice_in_dim(columns, col_index * part_rows, part_rows)
     pairs = [(n_col * a + b, n_col * b + a) for a in range(n_row) for b in range(n_col)]

time: 420 us -> 397 us (0.945)
  waiting for transfers between devices: 78.2 us -> 24.3 us
  blocking collectives: 0 us -> 30.2 us
    all_gather x1 -> x0, waiting for transfers between devices: 53.1 us -> none  [on_device(): columns = lax.all_gather(first_piece, 'col', axis=0, tiled=True)]
    all_to_all x0 -> x1, blocking collectives: none -> 30.2 us  [on_device(): columns = jnp.concatenate(lax.all_to_all(repeated, 'col', 0, 0), axis=0)]
  transfers between devices with their start and end apart: 18 -> 17, of which waited for: 7 -> 5; matrix products, arithmetic and copies ran while one was open for 21% -> 22% of each run, Pallas kernels for 0% -> 0%
where the time goes in v1:
time: 397 us; the launch traced here: 392 us
  other arithmetic  145 us (37%)
  local copies, waits for them, and re-layouts  91 us (23%)
  matrix products  43.5 us (11%)
  starting transfers between devices  42.3 us (11%)
  blocking collectives  30.2 us (8%)
  waiting for transfers between devices  24.3 us (6%)
  between operations  15.8 us (4%)
    another operation x12, other arithmetic, factor_and_invert(): factor[k, k] = jnp.linalg.cholesky(trailing[:size, :size])  50.4 us
    another operation x8, other arithmetic, factor_and_invert(): lax.linalg.triangular_solve(factor[k, k], eye, left_side=True, lower=True)  43.2 us
    all_to_all x1, blocking collectives, on_device(): columns = jnp.concatenate(lax.all_to_all(repeated, 'col', 0, 0), axis=0)  30.2 us
    sort x4, other arithmetic, select_rows(): chosen = jnp.argsort(keyed)[:count]  27 us
    gather x4, local copies, waits for them, and re-layouts, select_rows(): return parent_map[chosen] - owner * width  18.8 us
    ppermute x7, waiting for transfers between devices, on_device(): lax.ppermute(block_here[target * panel_rows:(target + 1) * panel_rows, :P...  15.2 us
    gather x2, local copies, waits for them, and re-layouts, on_device(): assembled = assembled + jnp.take(padded, row_lookup, axis=0)  14.1 us
    ppermute x7, starting transfers between devices, on_device(): lax.ppermute(block_here[target * panel_rows:(target + 1) * panel_rows, :P...  12.2 us
  transfers between devices with their start and end apart: 17, of which 5 were waited for; matrix products, arithmetic and copies ran while one was open for 22% of the time, Pallas kernels for 0%

profile of v1, /device:TPU:1, one launch (start us, length us, event | category | flops | bytes accessed | tf_op | source)
XLA Modules:
  0.0 392.4 jit_solution(5180303394732462482)
XLA Ops:
  8.8 4.4 %collective-permute-start.6 = (f32[128,512]{1,0:T(8,128)S(1)}, f32[128,512]{1,0:T(8,128)S(1)}, u32[]{:S(2)}, u32[]{:S(2)}) collective-permute-start(f32[128,512]{1,0:T(8,128)S(1)} %get-tuple-element.29), channel_id=1, source_target_pairs={{0,1},{8,9},{16,17},{24,25},{32,33},{40,41},{48,49},{56,57},{64,65... | collective-permute-start | bytes 786440 | tf_op jit(solution)/shard_map/ppermute | solution.py:106
  25.1 5.6 %collective-permute-done.3 = f32[128,512]{1,0:T(8,128)S(1)} collective-permute-done((f32[128,512]{1,0:T(8,128)S(1)}, f32[128,512]{1,0:T(8,128)S(1)}, u32[]{:S(2)}, u32[]{:S(2)}) %collective-permute-start.3) | collective-permute-done | bytes 262176 | tf_op jit(solution)/shard_map/ppermute | solution.py:106
  30.7 5.6 %collective-permute-done.2 = f32[128,512]{1,0:T(8,128)S(1)} collective-permute-done((f32[128,512]{1,0:T(8,128)S(1)}, f32[128,512]{1,0:T(8,128)S(1)}, u32[]{:S(2)}, u32[]{:S(2)}) %collective-permute-start.2) | collective-permute-done | bytes 262176 | tf_op jit(solution)/shard_map/ppermute | solution.py:106
  37.8 30.2 %all_to_all.14 = f32[8,128,512]{2,1,0:T(8,128)S(1)} all-to-all(f32[8,128,512]{2,1,0:T(8,128)S(1)} %stack.2), channel_id=1, replica_groups=mesh['child'=2,'row'=8,'col'=8] {'col'}, dimensions={0} | all-to-all | bytes 4194304 | tf_op jit(solution)/shard_map/all_to_all | solution.py:113
  76.0 11.4 %collective-permute-start.7 = (f32[128,512]{1,0:T(8,128)S(1)}, f32[128,512]{1,0:T(8,128)S(1)}, u32[]{:S(2)}, u32[]{:S(2)}) collective-permute-start(f32[128,512]{1,0:T(8,128)S(1)} %constant_dynamic-slice_fusion), channel_id=1, source_target_pairs={{0,0},{1,8},{2,16},{3,24},{4,32},{5,40},{6,48},{7,56},{8,1},{9,9},... | collective-permute-start | bytes 786440 | tf_op jit(solution)/shard_map/ppermute | solution.py:117
  99.1 8.5 %gather_fusion.1 = f32[1024,1024]{1,0:T(8,128)} fusion(f32[1024,1024]{1,0:T(8,128)} %bitcast.120, s32[1024]{0:T(1024)S(1)} %fusion.78), kind=kCustom, calls=%fused_computation.3 | custom fusion | bytes 8392704 | tf_op jit(solution)/shard_map/gather | solution.py:143
  108.2 7.0 %gather_fusion = pred[1024]{0:T(1024)(128)(4,1)S(1)} fusion(pred[1024]{0:T(1024)(128)(4,1)S(1)} %fusion.91, s32[1024]{0:T(1024)S(1)} %fusion.78), kind=kCustom, calls=%fused_computation.2 | custom fusion | bytes 6144 | tf_op jit(solution)/shard_map/gather | solution.py:146
  115.2 4.4 %sort.90 = (s32[1024]{0:T(1024)}, s32[1024]{0:T(1024)}) sort(s32[1024]{0:T(1024)S(1)} %get-tuple-element.62, s32[1024]{0:T(1024)S(1)} %iota.129), dimensions={0}, to_apply=%region_0.1 | sort | flops 10240 | bytes 16384 | tf_op jit(solution)/shard_map/jit(argsort)/sort | solution.py:138
  122.5 5.2 %all-gather.3.cloned.1.call-done = f32[1536,512]{1,0:T(8,128)} async-done(((f32[192,512]{1,0:T(8,128)}), f32[1536,512]{1,0:T(8,128)}) %all-gather.3.cloned.1.call-update) | async-done | bytes 3145744 | tf_op jit(solution)/shard_map/all_gather | solution.py:125
  132.9 11.7 %cholesky.74 = f32[128,128]{1,0:T(8,128)S(1)} custom-call(f32[128,128]{1,0:T(8,128)S(1)} %fusion.64), custom_call_target="Cholesky" | custom-call | tf_op jit(solution)/shard_map/jit(cholesky)/cholesky | solution.py:60
  146.1 9.8 %custom-call.8 = f32[1,128,128]{1,2,0:T(8,128)S(1)} custom-call(f32[1,128,128]{2,1,0:T(8,128)S(1)} %get-tuple-element.25), custom_call_target="InvertDiagBlocksLowerTriangular" | custom-call | tf_op jit(solution)/shard_map/triangular_solve/custom-call.0 | solution.py:61
  158.2 12.1 %cholesky.85 = f32[128,128]{1,0:T(8,128)S(1)} custom-call(f32[128,128]{1,0:T(8,128)S(1)} %fusion.62), custom_call_target="Cholesky" | custom-call | tf_op jit(solution)/shard_map/jit(cholesky)/cholesky | solution.py:60
  172.4 9.8 %custom-call.9 = f32[1,128,128]{1,2,0:T(8,128)S(1)} custom-call(f32[1,128,128]{2,1,0:T(8,128)S(1)} %get-tuple-element.23), custom_call_target="InvertDiagBlocksLowerTriangular" | custom-call | tf_op jit(solution)/shard_map/triangular_solve/custom-call.0 | solution.py:61
  184.1 11.7 %cholesky.96 = f32[128,128]{1,0:T(8,128)S(1)} custom-call(f32[128,128]{1,0:T(8,128)S(1)} %fusion.60), custom_call_target="Cholesky" | custom-call | tf_op jit(solution)/shard_map/jit(cholesky)/cholesky | solution.py:60
  197.7 9.8 %custom-call.10 = f32[1,128,128]{1,2,0:T(8,128)S(1)} custom-call(f32[1,128,128]{2,1,0:T(8,128)S(1)} %get-tuple-element.21), custom_call_target="InvertDiagBlocksLowerTriangular" | custom-call | tf_op jit(solution)/shard_map/triangular_solve/custom-call.0 | solution.py:61
  214.2 11.9 %cholesky.107 = f32[128,128]{1,0:T(8,128)S(1)} custom-call(f32[128,128]{1,0:T(8,128)S(1)} %fusion.58), custom_call_target="Cholesky" | custom-call | tf_op jit(solution)/shard_map/jit(cholesky)/cholesky | solution.py:60
  227.5 9.8 %custom-call.11 = f32[1,128,128]{1,2,0:T(8,128)S(1)} custom-call(f32[1,128,128]{2,1,0:T(8,128)S(1)} %get-tuple-element.19), custom_call_target="InvertDiagBlocksLowerTriangular" | custom-call | tf_op jit(solution)/shard_map/triangular_solve/custom-call.0 | solution.py:61
  241.1 5.8 %fusion.107 = f32[1024,512]{1,0:T(8,128)} fusion(f32[1024,512]{1,0:T(8,128)S(1)} %bitcast.135, f32[128,256]{1,0:T(8,128)S(1)} %broadcast.201, f32[128,128]{1,0:T(8,128)S(1)} %cholesky.75, f32[128,128]{1,0:T(8,128)S(1)} %fusion.45, f32[128,128]{1,0:T(8,128)S(1)} %copy.51, f32[128,128]{1,0:T(8,128)S(1)} %convolution_negate_fusion, ...), kind=kOutput, calls=%fused_computation.207 | convolution fusion | flops 3224633344 | bytes 5046272 | tf_op jit(solution)/shard_map/dot_general | solution.py:85
  247.2 4.9 %fusion.8 = f32[1024,512]{1,0:T(8,128)S(1)} fusion(f32[512,512]{1,0:T(8,128)S(1)} %fusion.21, f32[1024,512]{1,0:T(8,128)S(1)} %bitcast.132, pred[1024]{0:T(1024)(128)(4,1)S(1)} %copy-done.21, pred[1024]{0:T(1024)(128)(4,1)S(1)} %copy-done.22, f32[128,256]{1,0:T(8,128)S(1)} %broadcast.201, f32[128,128]{1,0:T(8,128)S(1)} %cholesky.75, ...), kind=kOutput, calls=%fused_computation.22 | convolution fusion | flops 3225681920 | bytes 6096896 | tf_op jit(solution)/shard_map/dot_general | solution.py:85
  252.1 4.9 %gather_fusion.2 = f32[1024,512]{1,0:T(8,128)} fusion(f32[1024,512]{1,0:T(8,128)S(1)} %fusion.8, s32[1024]{0:T(1024)S(1)} %fusion.78), kind=kCustom, calls=%fused_computation.4 | custom fusion | bytes 4198400 | tf_op jit(solution)/shard_map/gather | solution.py:144
  257.0 9.8 %fusion.10 = f32[1024,1024]{1,0:T(8,128)S(1)} fusion(f32[1024,512]{1,0:T(8,128)} %gather_fusion.2, f32[1024,512]{1,0:T(8,128)} %fusion.107, f32[512,512]{1,0:T(8,128)S(1)} %fusion.21, pred[1024]{0:T(1024)(128)(4,1)S(1)} %get-tuple-element.56, pred[1024]{0:T(1024)(128)(4,1)S(1)} %get-tuple-element.57), kind=kOutput, calls=%fused_computation.24 | convolution fusion | flops 6443499520 | bytes 9439232 | tf_op jit(solution)/shard_map/dot_general | solution.py:143
  266.9 9.0 %fusion.5 = f32[128,8,8,128]{3,1,2,0:T(8,128)S(1)} fusion(f32[1024,1024]{1,0:T(8,128)S(1)} %copy-done.4, f32[1024,1024]{1,0:T(8,128)S(1)} %fusion.10, s32[1024]{0:T(1024)S(1)} %copy-done.24, pred[1024]{0:T(1024)(128)(4,1)S(1)} %copy-done.23, pred[1024]{0:T(1024)(128)(4,1)S(1)} %gather_fusion), kind=kOutput, calls=%fused_computation.21 | convolution fusion | flops 12890144768 | bytes 12589056 | tf_op jit(solution)/shard_map/qj,iq->ji/dot_general | solution.py:147
  279.8 10.7 %all-to-all-start.1 = ((f32[128,64,128]{2,1,0:T(8,128)}), f32[128,64,128]{2,1,0:T(8,128)}, u32[]{:S(2)}, u32[]{:S(2)}) async-start(f32[128,64,128]{2,1,0:T(8,128)} %bitcast.122), calls=%async_computation.1 | async-start | bytes 8388608 | tf_op jit(solution)/shard_map/all_to_all | solution.py:154
  290.7 6.8 %sort.95 = (s32[8192]{0:T(1024)}, s32[8192]{0:T(1024)S(1)}) sort(s32[8192]{0:T(1024)S(1)} %get-tuple-element.54, s32[8192]{0:T(1024)S(1)} %iota.145), dimensions={0}, to_apply=%region_8.12 | sort | flops 106496 | bytes 131072 | tf_op jit(solution)/shard_map/jit(argsort)/sort | solution.py:34
  297.5 6.1 %gather_fusion.6 = s32[1024]{0:T(1024)S(1)} fusion(s32[8192]{0:T(1024)S(1)} %bitcast.116, s32[1024]{0:T(1024)S(1)} %fusion.80), kind=kCustom, calls=%fused_computation.8 | custom fusion | bytes 12288 | tf_op jit(solution)/shard_map/gather | solution.py:35
  303.6 6.8 %sort.94 = (s32[8192]{0:T(1024)}, s32[8192]{0:T(1024)S(1)}) sort(s32[8192]{0:T(1024)S(1)} %get-tuple-element.55, s32[8192]{0:T(1024)S(1)} %iota.143), dimensions={0}, to_apply=%region_7.11 | sort | flops 106496 | bytes 131072 | tf_op jit(solution)/shard_map/jit(argsort)/sort | solution.py:34
  313.6 6.8 %sort.92 = (s32[8192]{0:T(1024)}, s32[8192]{0:T(1024)S(1)}) sort(s32[8192]{0:T(1024)S(1)} %get-tuple-element.58, s32[8192]{0:T(1024)S(1)} %iota.138), dimensions={0}, to_apply=%region_4.7 | sort | flops 106496 | bytes 131072 | tf_op jit(solution)/shard_map/jit(argsort)/sort | solution.py:34
  323.7 6.8 %sort.93 = (s32[8192]{0:T(1024)}, s32[8192]{0:T(1024)S(1)}) sort(s32[8192]{0:T(1024)S(1)} %get-tuple-element.59, s32[8192]{0:T(1024)S(1)} %iota.140), dimensions={0}, to_apply=%region_5.8 | sort | flops 106496 | bytes 131072 | tf_op jit(solution)/shard_map/jit(argsort)/sort | solution.py:34
  330.5 6.1 %gather_fusion.4 = s32[1024]{0:T(1024)S(1)} fusion(s32[8192]{0:T(1024)S(1)} %bitcast.114, s32[1024]{0:T(1024)S(1)} %fusion.79), kind=kCustom, calls=%fused_computation.6 | custom fusion | bytes 12288 | tf_op jit(solution)/shard_map/gather | solution.py:35
  363.0 8.6 %gather_fusion.7 = f32[1536,768]{1,0:T(8,128)} fusion(f32[1025,768]{1,0:T(8,128)} %pad.15, s32[2048]{0:T(1024)S(1)} %pad_clamp_fusion.1), kind=kCustom, calls=%fused_computation.clone | custom fusion | bytes 9443328 | tf_op jit(solution)/shard_map/jit(_take)/gather | solution.py:172
  371.6 5.5 %gather_fusion.8 = f32[1536,768]{1,0:T(8,128)} fusion(f32[1025,768]{1,0:T(8,128)S(1)} %pad.16, s32[2048]{0:T(1024)S(1)} %pad_clamp_fusion), kind=kCustom, calls=%fused_computation.1.clone | custom fusion | bytes 9443328 | tf_op jit(solution)/shard_map/jit(_take)/gather | solution.py:172
  377.1 8.0 %select_add_fusion = f32[1536,768]{1,0:T(8,128)} fusion(f32[1536,768]{1,0:T(8,128)} %gather_fusion.8, f32[1536,768]{1,0:T(8,128)} %param.10, f32[1536,768]{1,0:T(8,128)} %gather_fusion.7, pred[1536]{0:T(1024)(128)(4,1)S(1)} %compare_and_fusion, pred[1536]{0:T(1024)(128)(4,1)S(1)} %compare_and_fusion.1), kind=kLoop, calls=%fused_computation.11 | loop fusion | flops 4718592 | bytes 18877440 | tf_op jit(solution)/shard_map/add | solution.py:172
  (206 shorter events, 100.8 us)
Async XLA Ops:
  7.2 120.5 %all-gather.3.cloned.1.call-start = ((), (), s32[]{:S(2)}) async-start(), calls=%async_computation.2 | async-start | bytes 3538944 | tf_op jit(solution)/shard_map/all_gather | solution.py:125
  8.8 9.7 %collective-permute-start.6 = (f32[128,512]{1,0:T(8,128)S(1)}, f32[128,512]{1,0:T(8,128)S(1)}, u32[]{:S(2)}, u32[]{:S(2)}) collective-permute-start(f32[128,512]{1,0:T(8,128)S(1)} %get-tuple-element.29), channel_id=1, source_target_pairs={{0,1},{8,9},{16,17},{24,25},{32,33},{40,41},{48,49},{56,57},{64,65... | collective-permute-start | bytes 786440 | tf_op jit(solution)/shard_map/ppermute | solution.py:106
  13.2 6.6 %collective-permute-start.5 = (f32[128,512]{1,0:T(8,128)S(1)}, f32[128,512]{1,0:T(8,128)S(1)}, u32[]{:S(2)}, u32[]{:S(2)}) collective-permute-start(f32[128,512]{1,0:T(8,128)S(1)} %get-tuple-element.30), channel_id=1, source_target_pairs={{0,2},{8,10},{16,18},{24,26},{32,34},{40,42},{48,50},{56,58},{64,6... | collective-permute-start | bytes 786440 | tf_op jit(solution)/shard_map/ppermute | solution.py:106
  14.5 10.6 %collective-permute-start.4 = (f32[128,512]{1,0:T(8,128)S(1)}, f32[128,512]{1,0:T(8,128)S(1)}, u32[]{:S(2)}, u32[]{:S(2)}) collective-permute-start(f32[128,512]{1,0:T(8,128)S(1)} %get-tuple-element.31), channel_id=1, source_target_pairs={{0,3},{8,11},{16,19},{24,27},{32,35},{40,43},{48,51},{56,59},{64,6... | collective-permute-start | bytes 786440 | tf_op jit(solution)/shard_map/ppermute | solution.py:106
  15.8 14.9 %collective-permute-start.3 = (f32[128,512]{1,0:T(8,128)S(1)}, f32[128,512]{1,0:T(8,128)S(1)}, u32[]{:S(2)}, u32[]{:S(2)}) collective-permute-start(f32[128,512]{1,0:T(8,128)S(1)} %get-tuple-element.32), channel_id=1, source_target_pairs={{0,4},{8,12},{16,20},{24,28},{32,36},{40,44},{48,52},{56,60},{64,6... | collective-permute-start | bytes 786440 | tf_op jit(solution)/shard_map/ppermute | solution.py:106
  17.1 19.2 %collective-permute-start.2 = (f32[128,512]{1,0:T(8,128)S(1)}, f32[128,512]{1,0:T(8,128)S(1)}, u32[]{:S(2)}, u32[]{:S(2)}) collective-permute-start(f32[128,512]{1,0:T(8,128)S(1)} %get-tuple-element.33), channel_id=1, source_target_pairs={{0,5},{8,13},{16,21},{24,29},{32,37},{40,45},{48,53},{56,61},{64,6... | collective-permute-start | bytes 786440 | tf_op jit(solution)/shard_map/ppermute | solution.py:106
  18.5 17.8 %collective-permute-start.1 = (f32[128,512]{1,0:T(8,128)S(1)}, f32[128,512]{1,0:T(8,128)S(1)}, u32[]{:S(2)}, u32[]{:S(2)}) collective-permute-start(f32[128,512]{1,0:T(8,128)S(1)} %get-tuple-element.34), channel_id=1, source_target_pairs={{0,6},{8,14},{16,22},{24,30},{32,38},{40,46},{48,54},{56,62},{64,7... | collective-permute-start | bytes 786440 | tf_op jit(solution)/shard_map/ppermute | solution.py:106
  19.8 16.5 %collective-permute-start = (f32[128,512]{1,0:T(8,128)S(1)}, f32[128,512]{1,0:T(8,128)S(1)}, u32[]{:S(2)}, u32[]{:S(2)}) collective-permute-start(f32[128,512]{1,0:T(8,128)S(1)} %get-tuple-element.35), channel_id=1, source_target_pairs={{0,7},{8,15},{16,23},{24,31},{32,39},{40,47},{48,55},{56,63},{64,7... | collective-permute-start | bytes 786440 | tf_op jit(solution)/shard_map/ppermute | solution.py:106
  68.0 24.3 %copy-start.2 = (f32[8,128,512]{2,1,0:T(8,128)}, f32[8,128,512]{2,1,0:T(8,128)S(1)}, u32[]{:S(2)}) copy-start(f32[8,128,512]{2,1,0:T(8,128)S(1)} %all_to_all.14) | copy-start | bytes 6291460
  68.0 24.3 %copy-start.25 = (s32[2]{0:T(128)S(1)}, s32[2]{0:T(128)}, u32[]{:S(2)}) copy-start(s32[2]{0:T(128)} %param.12) | copy-start | bytes 28
  68.1 5.3 %collective-permute-start.14 = (f32[64,512]{1,0:T(8,128)S(1)}, f32[64,512]{1,0:T(8,128)S(1)}, u32[]{:S(2)}, u32[]{:S(2)}) collective-permute-start(f32[64,512]{1,0:T(8,128)S(1)} %get-tuple-element.36), channel_id=1, source_target_pairs={{0,8},{1,9},{2,10},{3,11},{4,12},{5,13},{6,14},{7,15},{64,72},{65,... | collective-permute-start | bytes 393224 | tf_op jit(solution)/shard_map/ppermute | solution.py:121
  69.4 5.3 %collective-permute-start.13 = (f32[64,512]{1,0:T(8,128)S(1)}, f32[64,512]{1,0:T(8,128)S(1)}, u32[]{:S(2)}, u32[]{:S(2)}) collective-permute-start(f32[64,512]{1,0:T(8,128)S(1)} %get-tuple-element.37), channel_id=1, source_target_pairs={{0,16},{1,17},{2,18},{3,19},{4,20},{5,21},{6,22},{7,23},{64,80},{6... | collective-permute-start | bytes 393224 | tf_op jit(solution)/shard_map/ppermute | solution.py:121
  70.0 5.9 %collective-permute-start.12 = (f32[64,512]{1,0:T(8,128)S(1)}, f32[64,512]{1,0:T(8,128)S(1)}, u32[]{:S(2)}, u32[]{:S(2)}) collective-permute-start(f32[64,512]{1,0:T(8,128)S(1)} %get-tuple-element.38), channel_id=1, source_target_pairs={{0,24},{1,25},{2,26},{3,27},{4,28},{5,29},{6,30},{7,31},{64,88},{6... | collective-permute-start | bytes 393224 | tf_op jit(solution)/shard_map/ppermute | solution.py:121
  70.7 16.7 %collective-permute-start.11 = (f32[64,512]{1,0:T(8,128)S(1)}, f32[64,512]{1,0:T(8,128)}, u32[]{:S(2)}, u32[]{:S(2)}) collective-permute-start(f32[64,512]{1,0:T(8,128)S(1)} %get-tuple-element.39), channel_id=1, source_target_pairs={{0,32},{1,33},{2,34},{3,35},{4,36},{5,37},{6,38},{7,39},{64,96},{6... | collective-permute-start | bytes 393224 | tf_op jit(solution)/shard_map/ppermute | solution.py:121
  72.0 15.4 %collective-permute-start.10 = (f32[64,512]{1,0:T(8,128)S(1)}, f32[64,512]{1,0:T(8,128)}, u32[]{:S(2)}, u32[]{:S(2)}) collective-permute-start(f32[64,512]{1,0:T(8,128)S(1)} %get-tuple-element.40), channel_id=1, source_target_pairs={{0,40},{1,41},{2,42},{3,43},{4,44},{5,45},{6,46},{7,47},{64,104},{... | collective-permute-start | bytes 393224 | tf_op jit(solution)/shard_map/ppermute | solution.py:121
  73.3 14.1 %collective-permute-start.9 = (f32[64,512]{1,0:T(8,128)S(1)}, f32[64,512]{1,0:T(8,128)}, u32[]{:S(2)}, u32[]{:S(2)}) collective-permute-start(f32[64,512]{1,0:T(8,128)S(1)} %get-tuple-element.41), channel_id=1, source_target_pairs={{0,48},{1,49},{2,50},{3,51},{4,52},{5,53},{6,54},{7,55},{64,112},{... | collective-permute-start | bytes 393224 | tf_op jit(solution)/shard_map/ppermute | solution.py:121
  74.7 12.8 %collective-permute-start.8 = (f32[64,512]{1,0:T(8,128)S(1)}, f32[64,512]{1,0:T(8,128)}, u32[]{:S(2)}, u32[]{:S(2)}) collective-permute-start(f32[64,512]{1,0:T(8,128)S(1)} %get-tuple-element.42), channel_id=1, source_target_pairs={{0,56},{1,57},{2,58},{3,59},{4,60},{5,61},{6,62},{7,63},{64,120},{... | collective-permute-start | bytes 393224 | tf_op jit(solution)/shard_map/ppermute | solution.py:121
  76.0 15.5 %collective-permute-start.7 = (f32[128,512]{1,0:T(8,128)S(1)}, f32[128,512]{1,0:T(8,128)S(1)}, u32[]{:S(2)}, u32[]{:S(2)}) collective-permute-start(f32[128,512]{1,0:T(8,128)S(1)} %constant_dynamic-slice_fusion), channel_id=1, source_target_pairs={{0,0},{1,8},{2,16},{3,24},{4,32},{5,40},{6,48},{7,56},{8,1},{9,9},... | collective-permute-start | bytes 786440 | tf_op jit(solution)/shard_map/ppermute | solution.py:117
  210.7 30.2 %copy-start.5 = (f32[8,128,512]{2,1,0:T(8,128)S(1)}, f32[8,128,512]{2,1,0:T(8,128)}, u32[]{:S(2)}) copy-start(f32[8,128,512]{2,1,0:T(8,128)} %slice.219) | copy-start | bytes 6291460
  237.7 9.2 %copy-start.20 = (f32[128,128]{1,0:T(8,128)}, f32[128,128]{1,0:T(8,128)S(1)}, u32[]{:S(2)}) copy-start(f32[128,128]{1,0:T(8,128)S(1)} %copy.51) | copy-start | bytes 196612
  238.3 8.6 %copy-start.15 = (f32[128,128]{1,0:T(8,128)}, f32[128,128]{1,0:T(8,128)S(1)}, u32[]{:S(2)}) copy-start(f32[128,128]{1,0:T(8,128)S(1)} %convolution_negate_fusion.2) | copy-start | bytes 196612
  238.6 8.3 %copy-start.16 = (f32[128,128]{1,0:T(8,128)}, f32[128,128]{1,0:T(8,128)S(1)}, u32[]{:S(2)}) copy-start(f32[128,128]{1,0:T(8,128)S(1)} %convolution_negate_fusion) | copy-start | bytes 196612
  239.5 7.5 %copy-start.17 = (f32[128,128]{1,0:T(8,128)}, f32[128,128]{1,0:T(8,128)S(1)}, u32[]{:S(2)}) copy-start(f32[128,128]{1,0:T(8,128)S(1)} %convolution_negate_fusion.1) | copy-start | bytes 196612
  241.0 6.1 %copy-start.3 = (f32[8,128,512]{2,1,0:T(8,128)S(1)}, f32[8,128,512]{2,1,0:T(8,128)}, u32[]{:S(2)}) copy-start(f32[8,128,512]{2,1,0:T(8,128)} %copy-done.2) | copy-start | bytes 6291460
  241.0 6.1 %copy-start.18 = (f32[128,128]{1,0:T(8,128)S(1)}, f32[128,128]{1,0:T(8,128)}, u32[]{:S(2)}) copy-start(f32[128,128]{1,0:T(8,128)} %copy.44) | copy-start | bytes 196612
  241.0 6.1 %copy-start.19 = (f32[128,128]{1,0:T(8,128)S(1)}, f32[128,128]{1,0:T(8,128)}, u32[]{:S(2)}) copy-start(f32[128,128]{1,0:T(8,128)} %copy.47) | copy-start | bytes 196612
  241.1 6.1 %copy-start.21 = (pred[1024]{0:T(1024)(128)(4,1)S(1)}, pred[1024]{0:T(1024)(128)(4,1)}, u32[]{:S(2)}) copy-start(pred[1024]{0:T(1024)(128)(4,1)} %get-tuple-element.60) | copy-start | bytes 3076
  257.0 9.9 %copy-start.4 = (f32[1024,1024]{1,0:T(8,128)S(1)}, f32[1024,1024]{1,0:T(8,128)}, u32[]{:S(2)}) copy-start(f32[1024,1024]{1,0:T(8,128)} %gather_fusion.1) | copy-start | bytes 12582916
  257.0 9.9 %copy-start.23 = (pred[1024]{0:T(1024)(128)(4,1)S(1)}, pred[1024]{0:T(1024)(128)(4,1)}, u32[]{:S(2)}) copy-start(pred[1024]{0:T(1024)(128)(4,1)} %fusion.92) | copy-start | bytes 3076
  257.0 9.9 %copy-start.24 = (s32[1024]{0:T(1024)S(1)}, s32[1024]{0:T(1024)}, u32[]{:S(2)}) copy-start(s32[1024]{0:T(1024)} %get-tuple-element.11) | copy-start | bytes 12292
  279.8 10.7 %copy-start.14 = (s32[2,8192]{1,0:T(2,128)S(1)}, s32[2,8192]{1,0:T(2,128)}, u32[]{:S(2)}) copy-start(s32[2,8192]{1,0:T(2,128)} %param.11) | copy-start | bytes 196612
  279.8 65.7 %all-to-all-start.1 = ((f32[128,64,128]{2,1,0:T(8,128)}), f32[128,64,128]{2,1,0:T(8,128)}, u32[]{:S(2)}, u32[]{:S(2)}) async-start(f32[128,64,128]{2,1,0:T(8,128)} %bitcast.122), calls=%async_computation.1 | async-start | bytes 8388608 | tf_op jit(solution)/shard_map/all_to_all | solution.py:154
  (11 other events, 60.6 us)
Sparse Core Ops, SparseCore 0:
  92.4 35.2 all-gather.2
